TPU v7x, 512 devices: a whole 4x8x8 slice. The times are simulated.
512 devices in a mesh: wide: 64 (over y, z), narrow: 8 (over x, core).
Axes of the slice: x: 4, y: 8, z: 8, core: 2. Of those that a mesh axis runs over, the one named last changes fastest.
Arguments:
- amplitudes: bfloat16 [384, 2048], P('wide', 'narrow'), may hold values from -6 to 6
- integrals: bfloat16 [262144, 2048], P('wide', 'narrow'), may hold values from -0.375 to 0.375
- virtual_irrep: int32 [512], replicated, may hold values from 0 to 7
- column_irrep: int32 [2048], P('narrow'), may hold values from 0 to 7
- pair_energy: float32 [384], P('narrow'), may hold values from -4 to -1
- virtual_energy: float32 [512], replicated, may hold values from 0.5 to 3
- residual_in: bfloat16 [384, 262144], P('narrow', 'wide'), may hold values from -6 to 6
Outputs:
- new_amplitudes: bfloat16 [384, 262144], P('narrow', 'wide')
All inputs are finite; a program needn't handle non-finite values.
Results may differ from a plain program's by a relative error of at most 0.012.
Values may be sent and summed in bfloat16 or wider, within the bound.
No kernel may reach another device: no remote copies, remote signals or barrier semaphores. Data moves between devices by JAX's collectives and lax.ppermute only.
A program may use at most 64 MiB of HBM per device.

v0:
```python
import jax
import jax.numpy as jnp
from jax import lax
from jax.sharding import PartitionSpec as P


def local(
    amplitudes, integrals, virtual_irrep, column_irrep, pair_energy, virtual_energy, residual_in
):
    wide_size = lax.axis_size("wide")
    num_virt = virtual_irrep.shape[0]
    a_local = num_virt // wide_size
    first_a = lax.axis_index("wide") * a_local
    local_irrep = lax.dynamic_slice_in_dim(virtual_irrep, first_a, a_local, 0)
    row_irrep = jnp.bitwise_xor(local_irrep[:, None], virtual_irrep[None, :]).reshape(
        a_local * num_virt
    )
    masked = jnp.where(
        row_irrep[:, None] == column_irrep[None, :], integrals, jnp.zeros((), integrals.dtype)
    )
    contract = (((1,), (1,)), ((), ()))
    terms = lax.dot_general(
        lax.all_gather(amplitudes, "wide", axis=0, tiled=True),
        masked,
        contract,
        preferred_element_type=jnp.float32,
    )
    ladder = lax.psum_scatter(
        terms.astype(jnp.bfloat16), "narrow", scatter_dimension=0, tiled=True
    ).astype(jnp.float32)
    pair_rows = ladder.shape[0]
    ladder_cube = ladder.reshape(pair_rows, a_local, num_virt)
    swapped = lax.all_to_all(
        ladder_cube.astype(jnp.bfloat16), "wide", split_axis=2, concat_axis=2, tiled=True
    ).astype(ladder_cube.dtype)
    mirrored = swapped.reshape(pair_rows, a_local, wide_size, a_local)
    mirrored = jnp.transpose(mirrored, (0, 3, 2, 1)).reshape(pair_rows, a_local * num_virt)
    local_energy = lax.dynamic_slice_in_dim(virtual_energy, first_a, a_local, 0)
    denominator = (
        pair_energy[:, None, None] - local_energy[None, :, None] - virtual_energy[None, None, :]
    )
    denominator = denominator.reshape(pair_rows, a_local * num_virt)
    total = residual_in.astype(jnp.float32) + ladder - mirrored
    return (total / denominator).astype(jnp.bfloat16)


def solution(mesh):
    return jax.shard_map(
        local,
        mesh=mesh,
        in_specs=(
            P("wide", "narrow"),
            P("wide", "narrow"),
            P(),
            P("narrow"),
            P("narrow"),
            P(),
            P("narrow", "wide"),
        ),
        out_specs=P("narrow", "wide"),
        check_vma=False,
    )
```

profile of v0, /device:TPU:23, one launch (start us, length us, event | category | flops | bytes accessed | tf_op | source)
XLA Modules:
  0.0 151.3 jit_solution(6612598673634443218)
XLA Ops:
  6.5 0.0 reduce-scatter.4.cloned.1.call-start
  6.5 0.8 dynamic_slice.6
  7.3 0.8 xor_bitcast_fusion
  8.1 44.1 %all-gather = bf16[64,6,256]{2,1,0:T(8,128)(2,1)S(1)} all-gather(bf16[1,6,256]{2,1,0:T(8,128)(2,1)} %bitcast.31), channel_id=1, replica_groups=mesh['wide'=64,'narrow'=8] {'wide'}, dimensions={0}, use_global_device_ids=true | all-gather | bytes 199680 | tf_op jit(solution)/shard_map/all_gather | solution.py:23
  52.1 0.1 reshape.74
  52.2 2.8 %fusion = bf16[384,4096]{0,1:T(8,128)(2,1)S(1)} fusion(bf16[384,256]{1,0:T(8,128)(2,1)S(1)} %reshape.74, bf16[4096,256]{1,0:T(8,128)(2,1)} %param.8, s32[256]{0:T(256)} %param.10, s32[4096]{0:T(1024)S(1)} %bitcast.30), kind=kOutput, calls=%fused_computation.1 | convolution fusion | flops 808976384 | bytes 5456896 | tf_op jit(solution)/shard_map/dot_general | solution.py:22
  55.0 2.9 %copy.25 = bf16[384,4096]{1,0:T(8,128)(2,1)} copy(bf16[384,4096]{0,1:T(8,128)(2,1)S(1)} %fusion) | data formatting | bytes 6291456
  57.9 0.0 reduce-scatter.4.cloned.1.call-update
  57.9 47.4 %reduce-scatter.4.cloned.1.call-done = bf16[48,4096]{1,0:T(8,128)(2,1)} async-done(((bf16[384,4096]{1,0:T(8,128)(2,1)}), bf16[48,4096]{1,0:T(8,128)(2,1)}) %reduce-scatter.4.cloned.1.call-update) | async-done | bytes 393232 | tf_op jit(solution)/shard_map/reduce_scatter | solution.py:28
  105.4 1.5 copy.26
  106.8 0.0 copy-start.2
  106.8 0.0 copy-start.3
  106.9 0.7 copy.31
  107.5 2.5 %reshape.77 = bf16[64,2,1536]{2,1,0:T(2,128)(2,1)} reshape(bf16[512,8,48]{2,1,0:T(8,128)(2,1)S(1)} %bitcast.25) | data formatting | bytes 786432
  110.0 12.8 %all-to-all-start = ((bf16[64,2,1536]{2,1,0:T(2,128)(2,1)}), bf16[64,2,1536]{2,1,0:T(2,128)(2,1)S(1)}, u32[]{:S(2)}, u32[]{:S(2)}) async-start(bf16[64,2,1536]{2,1,0:T(2,128)(2,1)} %reshape.77), calls=%async_computation | async-start | bytes 786432 | tf_op jit(solution)/shard_map/all_to_all | solution.py:33
  122.8 0.0 copy-done.2
  122.9 0.1 dynamic_slice.7
  122.9 0.0 copy-done.3
  122.9 0.1 broadcast_subtract_fusion
  123.0 0.1 sub.45
  123.1 1.3 copy.28
  124.5 15.1 %all-to-all-done = bf16[64,2,1536]{2,1,0:T(2,128)(2,1)S(1)} async-done(((bf16[64,2,1536]{2,1,0:T(2,128)(2,1)}), bf16[64,2,1536]{2,1,0:T(2,128)(2,1)S(1)}, u32[]{:S(2)}, u32[]{:S(2)}) %all-to-all-start) | async-done | bytes 393248 | tf_op jit(solution)/shard_map/all_to_all | solution.py:33
  139.6 1.0 reshape.78
  140.6 0.1 copy.23
  140.8 0.0 copy-start
  140.8 0.0 copy-start.1
  140.8 1.5 copy.24
  142.3 0.0 copy-done
  142.3 0.0 copy-done.1
  142.3 2.2 %divide_convert_fusion = bf16[48,4096]{1,0:T(8,128)(2,1)} fusion(f32[48,4096]{1,0:T(8,128)S(1)} %bitcast.28, f32[48,4096]{1,0:T(8,128)} %copy.24, bf16[48,4096]{1,0:T(8,128)(2,1)S(1)} %copy-done.1, bf16[48,4096]{1,0:T(8,128)(2,1)} %param.13, f32[4096]{0:T(1024)S(1)} %bitcast.29), kind=kLoop, calls=%fused_computation.6 | loop fusion | flops 1376256 | bytes 2768896 | tf_op jit(solution)/shard_map/convert_element_type | solution.py:44
  (3 shorter events, 0.0 us)
Async XLA Ops:
  6.5 98.8 %reduce-scatter.4.cloned.1.call-start = ((), (), s32[]{:S(2)}) async-start(), calls=%async_computation.2 | async-start | bytes 3538944 | tf_op jit(solution)/shard_map/reduce_scatter | solution.py:28
  106.8 16.0 %copy-start.2 = (f32[512]{0:T(512)S(1)}, f32[512]{0:T(512)}, u32[]{:S(2)}) copy-start(f32[512]{0:T(512)} %param.12) | copy-start | bytes 6148
  106.8 16.1 %copy-start.3 = (f32[48]{0:T(128)S(1)}, f32[48]{0:T(128)}, u32[]{:S(2)}) copy-start(f32[48]{0:T(128)} %param.11) | copy-start | bytes 580
  110.0 29.6 %all-to-all-start = ((bf16[64,2,1536]{2,1,0:T(2,128)(2,1)}), bf16[64,2,1536]{2,1,0:T(2,128)(2,1)S(1)}, u32[]{:S(2)}, u32[]{:S(2)}) async-start(bf16[64,2,1536]{2,1,0:T(2,128)(2,1)} %reshape.77), calls=%async_computation | async-start | bytes 786432 | tf_op jit(solution)/shard_map/all_to_all | solution.py:33
  140.8 1.5 copy-start
  140.8 1.5 copy-start.1
Sparse Core Ops, SparseCore 0:
  58.1 47.2 reduce-scatter.3
where the time goes:
time: 152 us; the launch traced here: 151 us
  waiting for transfers between devices  62.5 us (41%)
  blocking collectives  44.1 us (29%)
  between operations  13.5 us (9%)
  starting transfers between devices  12.8 us (8%)
  local copies, waits for them, and re-layouts  12.6 us (8%)
  other arithmetic  3 us (2%)
  matrix products  2.8 us (2%)
    reduce_scatter x1, waiting for transfers between devices, local(): lax.psum_scatter(terms.astype(jnp.bfloat16), 'narrow', scatter_dimension=...  47.4 us
    all_gather x1, blocking collectives, local(): lax.all_gather(amplitudes, 'wide', axis=0, tiled=True)  44.1 us
    all_to_all x1, waiting for transfers between devices, local(): lax.all_to_all(ladder_cube.astype(jnp.bfloat16), 'wide', split_axis=2, co...  15.1 us
    all_to_all x1, starting transfers between devices, local(): lax.all_to_all(ladder_cube.astype(jnp.bfloat16), 'wide', split_axis=2, co...  12.8 us
    unnamed x17, local copies, waits for them, and re-layouts  9.39 us
  transfers between devices with their start and end apart: 2, of which 2 were waited for; matrix products, arithmetic and copies ran while one was open for 1% of the time, Pallas kernels for 0%

commit v1 on v0

--- a/solution.py
+++ b/solution.py
@@ -2,6 +2,7 @@
 import jax.numpy as jnp
 from jax import lax
 from jax.sharding import PartitionSpec as P
+from jax.lax import all_to_all, axis_size
 
 
 def local(
@@ -19,8 +20,11 @@
         row_irrep[:, None] == column_irrep[None, :], integrals, jnp.zeros((), integrals.dtype)
     )
     contract = (((1,), (1,)), ((), ()))
+    hold_things = lambda block_in, comm_axis: jnp.concatenate(
+        all_to_all(jnp.stack([block_in] * axis_size(comm_axis)), comm_axis, 0, 0), axis=0
+    )
     terms = lax.dot_general(
-        lax.all_gather(amplitudes, "wide", axis=0, tiled=True),
+        hold_things(amplitudes, comm_axis="wide"),
         masked,
         contract,
         preferred_element_type=jnp.float32,

time: 152 us -> 123 us (0.81)
  blocking collectives: 44.1 us -> 0 us
  starting transfers between devices: 12.8 us -> 28.8 us
  waiting for transfers between devices: 62.5 us -> 60.6 us
    all_gather x1 -> x0, blocking collectives: 44.1 us -> none  [local(): lax.all_gather(amplitudes, 'wide', axis=0, tiled=True)]
    all_to_all x0 -> x1, starting transfers between devices: none -> 15.9 us  [local(): all_to_all(jnp.stack([block_in] * axis_size(comm_axis)), comm_axis, 0, 0)]
    reduce_scatter x1, waiting for transfers between devices: 47.4 us -> 33.9 us  [local(): lax.psum_scatter(terms.astype(jnp.bfloat16), 'narrow', scatter_dimension=...]
    all_to_all x0 -> x1, waiting for transfers between devices: none -> 11.6 us  [local(): all_to_all(jnp.stack([block_in] * axis_size(comm_axis)), comm_axis, 0, 0)]
    unnamed x17 -> x16, local copies, waits for them, and re-layouts: 9.39 us -> 9.33 us
  transfers between devices with their start and end apart: 2 -> 3, of which waited for: 2 -> 3; matrix products, arithmetic and copies ran while one was open for 1% -> 3% of each run, Pallas kernels for 0% -> 0%
where the time goes in v1:
time: 123 us
  waiting for transfers between devices  60.6 us (49%)
  starting transfers between devices  28.8 us (23%)
  local copies, waits for them, and re-layouts  14 us (11%)
  between operations  13.5 us (11%)
  other arithmetic  3 us (2%)
  matrix products  2.79 us (2%)
    reduce_scatter x1, waiting for transfers between devices, local(): lax.psum_scatter(terms.astype(jnp.bfloat16), 'narrow', scatter_dimension=...  33.9 us
    all_to_all x1, starting transfers between devices, local(): all_to_all(jnp.stack([block_in] * axis_size(comm_axis)), comm_axis, 0, 0)  15.9 us
    all_to_all x1, waiting for transfers between devices, local(): lax.all_to_all(ladder_cube.astype(jnp.bfloat16), 'wide', split_axis=2, co...  15.1 us
    all_to_all x1, starting transfers between devices, local(): lax.all_to_all(ladder_cube.astype(jnp.bfloat16), 'wide', split_axis=2, co...  12.8 us
    all_to_all x1, waiting for transfers between devices, local(): all_to_all(jnp.stack([block_in] * axis_size(comm_axis)), comm_axis, 0, 0)  11.6 us
    unnamed x16, local copies, waits for them, and re-layouts  9.33 us
    dot_general x1, matrix products, local(): lax.dot_general(hold_things(amplitudes, comm_axis='wide'), masked, contra...  2.79 us
  transfers between devices with their start and end apart: 3, of which 3 were waited for; matrix products, arithmetic and copies ran while one was open for 3% of the time, Pallas kernels for 0%

profile of v1, /device:TPU:23, one launch (start us, length us, event | category | flops | bytes accessed | tf_op | source)
XLA Modules:
  0.0 122.7 jit_solution(12665315649769780214)
XLA Ops:
  6.5 1.4 %stack.2 = bf16[64,6,256]{2,1,0:T(8,128)(2,1)} broadcast(bf16[6,256]{1,0:T(8,128)(2,1)} %param.7), dimensions={1,2} | broadcast | bytes 199680 | tf_op jit(solution)/shard_map/stack | solution.py:24
  7.9 15.9 %all-to-all-start = ((bf16[64,6,256]{2,1,0:T(8,128)(2,1)}), bf16[64,6,256]{2,1,0:T(8,128)(2,1)S(1)}, u32[]{:S(2)}, u32[]{:S(2)}) async-start(bf16[64,6,256]{2,1,0:T(8,128)(2,1)} %stack.2), calls=%async_computation | async-start | bytes 524288 | tf_op jit(solution)/shard_map/all_to_all | solution.py:24
  23.9 0.0 reduce-scatter.4.cloned.1.call-start
  23.9 0.8 dynamic_slice.6
  24.7 0.8 xor_bitcast_fusion
  25.4 11.6 %all-to-all-done = bf16[64,6,256]{2,1,0:T(8,128)(2,1)S(1)} async-done(((bf16[64,6,256]{2,1,0:T(8,128)(2,1)}), bf16[64,6,256]{2,1,0:T(8,128)(2,1)S(1)}, u32[]{:S(2)}, u32[]{:S(2)}) %all-to-all-start) | async-done | bytes 196640 | tf_op jit(solution)/shard_map/all_to_all | solution.py:24
  37.0 0.1 reshape.70
  37.1 2.8 %fusion = bf16[384,4096]{0,1:T(8,128)(2,1)S(1)} fusion(bf16[384,256]{1,0:T(8,128)(2,1)S(1)} %reshape.70, bf16[4096,256]{1,0:T(8,128)(2,1)} %param.8, s32[256]{0:T(256)} %param.10, s32[4096]{0:T(1024)S(1)} %bitcast.29), kind=kOutput, calls=%fused_computation.1 | convolution fusion | flops 808976384 | bytes 5456896 | tf_op jit(solution)/shard_map/dot_general | solution.py:26
  39.9 2.9 %copy.25 = bf16[384,4096]{1,0:T(8,128)(2,1)} copy(bf16[384,4096]{0,1:T(8,128)(2,1)S(1)} %fusion) | data formatting | bytes 6291456
  42.8 0.0 reduce-scatter.4.cloned.1.call-update
  42.8 33.9 %reduce-scatter.4.cloned.1.call-done = bf16[48,4096]{1,0:T(8,128)(2,1)} async-done(((bf16[384,4096]{1,0:T(8,128)(2,1)}), bf16[48,4096]{1,0:T(8,128)(2,1)}) %reduce-scatter.4.cloned.1.call-update) | async-done | bytes 393232 | tf_op jit(solution)/shard_map/reduce_scatter | solution.py:32
  76.8 1.5 %copy.26 = bf16[48,4096]{0,1:T(8,128)(2,1)S(1)} copy(bf16[48,4096]{1,0:T(8,128)(2,1)} %reduce-scatter.4.cloned.1.call-done) | data formatting | bytes 786432
  78.2 0.0 copy-start.2
  78.3 0.0 copy-start.3
  78.3 0.7 copy.31
  79.0 2.5 %reshape.81 = bf16[64,2,1536]{2,1,0:T(2,128)(2,1)} reshape(bf16[512,8,48]{2,1,0:T(8,128)(2,1)S(1)} %bitcast.24) | data formatting | bytes 786432
  81.4 12.8 %all-to-all-start.1 = ((bf16[64,2,1536]{2,1,0:T(2,128)(2,1)}), bf16[64,2,1536]{2,1,0:T(2,128)(2,1)S(1)}, u32[]{:S(2)}, u32[]{:S(2)}) async-start(bf16[64,2,1536]{2,1,0:T(2,128)(2,1)} %reshape.81), calls=%async_computation.1 | async-start | bytes 786432 | tf_op jit(solution)/shard_map/all_to_all | solution.py:37
  94.2 0.0 copy-done.2
  94.3 0.1 dynamic_slice.7
  94.3 0.0 copy-done.3
  94.3 0.1 broadcast_subtract_fusion
  94.4 0.1 sub.45
  94.5 1.4 %copy.28 = f32[6,8,8,512]{3,1,2,0:T(8,128)} copy(f32[6,8,8,512]{3,2,1,0:T(8,128)S(1)} %bitcast.26) | data formatting | bytes 1572864
  95.9 15.1 %all-to-all-done.1 = bf16[64,2,1536]{2,1,0:T(2,128)(2,1)S(1)} async-done(((bf16[64,2,1536]{2,1,0:T(2,128)(2,1)}), bf16[64,2,1536]{2,1,0:T(2,128)(2,1)S(1)}, u32[]{:S(2)}, u32[]{:S(2)}) %all-to-all-start.1) | async-done | bytes 393248 | tf_op jit(solution)/shard_map/all_to_all | solution.py:37
  111.0 1.0 reshape.82
  112.1 0.1 copy.23
  112.2 0.0 copy-start
  112.2 0.0 copy-start.1
  112.2 1.5 %copy.24 = f32[48,4096]{1,0:T(8,128)} copy(f32[48,4096]{0,1:T(8,128)S(1)} %bitcast.22) | data formatting | bytes 1572864 | tf_op jit(solution)/shard_map/reshape | solution.py:41
  113.7 0.0 copy-done
  113.7 0.0 copy-done.1
  113.7 2.2 %divide_convert_fusion = bf16[48,4096]{1,0:T(8,128)(2,1)} fusion(f32[48,4096]{1,0:T(8,128)S(1)} %bitcast.27, f32[48,4096]{1,0:T(8,128)} %copy.24, bf16[48,4096]{1,0:T(8,128)(2,1)S(1)} %copy-done.1, bf16[48,4096]{1,0:T(8,128)(2,1)} %param.13, f32[4096]{0:T(1024)S(1)} %bitcast.28), kind=kLoop, calls=%fused_computation.6 | loop fusion | flops 1376256 | bytes 2768896 | tf_op jit(solution)/shard_map/convert_element_type | solution.py:48
  (3 shorter events, 0.0 us)
Async XLA Ops:
  7.9 29.1 %all-to-all-start = ((bf16[64,6,256]{2,1,0:T(8,128)(2,1)}), bf16[64,6,256]{2,1,0:T(8,128)(2,1)S(1)}, u32[]{:S(2)}, u32[]{:S(2)}) async-start(bf16[64,6,256]{2,1,0:T(8,128)(2,1)} %stack.2), calls=%async_computation | async-start | bytes 524288 | tf_op jit(solution)/shard_map/all_to_all | solution.py:24
  23.9 52.9 %reduce-scatter.4.cloned.1.call-start = ((), (), s32[]{:S(2)}) async-start(), calls=%async_computation.3 | async-start | bytes 3538944 | tf_op jit(solution)/shard_map/reduce_scatter | solution.py:32
  78.2 16.0 %copy-start.2 = (f32[512]{0:T(512)S(1)}, f32[512]{0:T(512)}, u32[]{:S(2)}) copy-start(f32[512]{0:T(512)} %param.12) | copy-start | bytes 6148
  78.3 16.1 %copy-start.3 = (f32[48]{0:T(128)S(1)}, f32[48]{0:T(128)}, u32[]{:S(2)}) copy-start(f32[48]{0:T(128)} %param.11) | copy-start | bytes 580
  81.4 29.6 %all-to-all-start.1 = ((bf16[64,2,1536]{2,1,0:T(2,128)(2,1)}), bf16[64,2,1536]{2,1,0:T(2,128)(2,1)S(1)}, u32[]{:S(2)}, u32[]{:S(2)}) async-start(bf16[64,2,1536]{2,1,0:T(2,128)(2,1)} %reshape.81), calls=%async_computation.1 | async-start | bytes 786432 | tf_op jit(solution)/shard_map/all_to_all | solution.py:37
  112.2 1.5 %copy-start = (f32[6,8,8,512]{3,1,2,0:T(8,128)S(1)}, f32[6,8,8,512]{3,1,2,0:T(8,128)}, u32[]{:S(2)}) copy-start(f32[6,8,8,512]{3,1,2,0:T(8,128)} %copy.28) | copy-start | bytes 2359300
  112.2 1.5 %copy-start.1 = (bf16[48,4096]{1,0:T(8,128)(2,1)S(1)}, bf16[48,4096]{1,0:T(8,128)(2,1)}, u32[]{:S(2)}) copy-start(bf16[48,4096]{1,0:T(8,128)(2,1)} %reduce-scatter.4.cloned.1.call-done) | copy-start | bytes 1179652
Sparse Core Ops, SparseCore 0:
  43.0 33.7 reduce-scatter.3
